TPU v7x, 128 devices: a whole 4x4x4 slice. The times are simulated.
128 devices in a mesh: seq: 32 (over y, x, z_lo), chan: 4 (over z_hi, core).
Axes of the slice: x: 4, y: 4, z: 4 (z_hi: 2, z_lo: 2; z = z_hi * 2 + z_lo), core: 2. Of those that a mesh axis runs over, the one named last changes fastest.
Arguments:
- tokens: bfloat16 [24576, 4096], P('seq', 'chan'), may hold values from -4 to 4
- w_in: bfloat16 [8, 4096, 1296], P('chan', 'seq'), may hold values from -1 to 1
- conv_w: float32 [8, 4, 1280], P('chan'), may hold values from -3 to 3
- conv_b: float32 [8, 1280], P('chan'), may hold values from -3 to 3
- dt_bias: float32 [8, 16], P('chan'), may hold values from -8 to 2
- a_log: float32 [8, 16], P('chan'), may hold values from -4.6 to -3.7
- d_skip: float32 [8, 16], P('chan'), may hold values from 0.3 to 3
- norm_gain: float32 [8, 1024], P('chan'), may hold values from 0.5 to 1.5
Outputs:
- mixer_out: bfloat16 [24576, 8192], P('seq', 'chan')
All inputs are finite; a program needn't handle non-finite values.
Results may differ from a plain program's by a relative error of at most 0.0076.
Values may be sent and summed in bfloat16 or wider, within the bound.
No kernel may reach another device: no remote copies, remote signals or barrier semaphores. Data moves between devices by JAX's collectives and lax.ppermute only.
A program may use at most 128 MiB of HBM per device.

v0:
```python
import jax
import jax.numpy as jnp
from jax import lax
from jax.sharding import PartitionSpec as P

P_SIZE = 64
N = 128
KCONV = 4
Q = 128
HG = 16
GW = 1024
CW = 1280
epsilon = 1e-05


def shifted(block, axis, distance):
    devices = range(lax.axis_size(axis))
    route = [(i - distance, i) for i in devices if i - distance in devices]
    return lax.ppermute(block, axis, route)


def entering(keep, end, axis):
    place = lax.axis_index(axis)
    size = lax.axis_size(axis)
    keep = jnp.where(place == 0, 1.0, shifted(keep, axis, 1))
    end = shifted(end, axis, 1)
    distance = 1
    while distance < size:
        earlier_end = shifted(end, axis, distance)
        reach = place >= distance
        end = jnp.where(reach, keep[..., None, None] * earlier_end + end, end)
        if distance * 2 < size:
            earlier_keep = shifted(keep, axis, distance)
            keep = jnp.where(reach, keep * earlier_keep, keep)
        distance *= 2
    return end


def mix_groups(gathered, w_in, conv_w, conv_b, dt_bias, a_log, d_skip, norm_gain):
    groups = w_in.shape[0]
    row_count = gathered.shape[0]
    rows_first = jnp.transpose(w_in, (1, 0, 2))
    full_w = lax.all_gather(rows_first, "seq", axis=0, tiled=True)
    projected = jnp.einsum("td,dgc->tgc", gathered, full_w, preferred_element_type=jnp.float32)
    conv_in = projected[:, :, :CW].astype(jnp.bfloat16)
    raw_dt = projected[:, :, CW:]
    rim_rows = shifted(conv_in[row_count - (KCONV - 1) :], "seq", 1)
    padded = jnp.concatenate([rim_rows, conv_in], axis=0)
    pre_act = jnp.broadcast_to(conv_b[None], (row_count, groups, CW))
    for offset in range(KCONV):
        pre_act = pre_act + conv_w[None, :, offset] * padded[offset : offset + row_count]
    inputs = jax.nn.silu(pre_act).astype(jnp.bfloat16)
    block_count = row_count // Q
    blocked = inputs.reshape(block_count, Q, groups, CW)
    x_all = blocked[..., :GW].reshape(block_count, Q, groups, HG, P_SIZE)
    b_all = blocked[..., GW : GW + N]
    c_all = blocked[..., GW + N :]
    step_dt = jax.nn.softplus(raw_dt + dt_bias[None]).reshape(block_count, Q, groups, HG)
    decay_rate = -jnp.exp(a_log)
    cumulative = jnp.cumsum(decay_rate[None, None] * step_dt, axis=1)
    causal = lax.broadcasted_iota(jnp.int32, (Q, Q), 0) >= lax.broadcasted_iota(
        jnp.int32, (Q, Q), 1
    )
    last_cum = cumulative[:, -1]
    keep_all = jnp.exp(last_cum)
    tail_factor = jnp.exp(last_cum[:, None] - cumulative) * step_dt
    scaled = (x_all * tail_factor[..., None]).astype(jnp.bfloat16)
    fresh_all = jnp.einsum("qjghp,qjgn->qghpn", scaled, b_all, preferred_element_type=jnp.float32)
    local_states = []
    state_now = jnp.zeros(fresh_all.shape[1:], jnp.float32)
    keep_now = jnp.ones(keep_all.shape[1:], jnp.float32)
    keep_before = []
    for q in range(block_count):
        local_states.append(state_now)
        keep_before.append(keep_now)
        state_now = keep_all[q][..., None, None] * state_now + fresh_all[q]
        keep_now = keep_now * keep_all[q]
    incoming = entering(keep_now, state_now, "seq")
    states = jnp.stack(local_states) + jnp.stack(keep_before)[..., None, None] * incoming[None]
    scores = jnp.einsum("qign,qjgn->qgij", c_all, b_all, preferred_element_type=jnp.float32)
    cum_cols = jnp.transpose(cumulative, (0, 2, 3, 1))
    dt_cols = jnp.transpose(step_dt, (0, 2, 3, 1))
    spread = cum_cols[..., :, None] - cum_cols[..., None, :]
    damping = jnp.where(causal, jnp.exp(jnp.minimum(spread, 0.0)), 0.0)
    weights = (scores[:, :, None] * damping * dt_cols[..., None, :]).astype(jnp.bfloat16)
    partial_y = jnp.einsum("qghij,qjghp->qighp", weights, x_all, preferred_element_type=jnp.float32)
    partial_y = partial_y + d_skip[None, None, :, :, None] * x_all
    across = jnp.einsum(
        "qign,qghpn->qighp", c_all, states.astype(jnp.bfloat16), preferred_element_type=jnp.float32
    )
    activity = partial_y + jnp.exp(cumulative)[..., None] * across
    flat_act = activity.reshape(row_count, groups, GW)
    inv_rms = lax.rsqrt(jnp.mean(flat_act * flat_act, axis=-1, keepdims=True) + epsilon)
    normed = (flat_act * inv_rms * norm_gain[None]).astype(jnp.bfloat16)
    return normed.reshape(row_count, groups * GW)


def per_device(tokens, w_in, conv_w, conv_b, dt_bias, a_log, d_skip, norm_gain):
    gathered = lax.all_gather(tokens, "chan", axis=1, tiled=True)
    return mix_groups(gathered, w_in, conv_w, conv_b, dt_bias, a_log, d_skip, norm_gain)


def solution(mesh):
    return jax.shard_map(
        per_device,
        mesh=mesh,
        in_specs=(
            P("seq", "chan"),
            P("chan", "seq", None),
            P("chan", None, None),
            P("chan", None),
            P("chan", None),
            P("chan", None),
            P("chan", None),
            P("chan", None),
        ),
        out_specs=P("seq", "chan"),
        check_vma=False,
    )
```

profile of v0, /device:TPU:80, one launch (start us, length us, event | category | flops | bytes accessed | tf_op | source)
XLA Modules:
  0.0 843.2 jit_solution(2859440067428863867)
XLA Ops:
  9.7 48.6 %all-gather.3.cloned.1.call-done = bf16[768,4096]{1,0:T(8,128)(2,1)} async-done(((bf16[768,1024]{1,0:T(8,128)(2,1)}), bf16[768,4096]{1,0:T(8,128)(2,1)}) %all-gather.3.cloned.1.call-update) | async-done | bytes 6291472 | tf_op jit(solution)/shard_map/all_gather | solution.py:99
  58.3 513.7 %all-gather.5.cloned.1.call-done = bf16[4096,2,1296]{0,2,1:T(8,128)(2,1)} async-done(((bf16[128,2,1296]{0,2,1:T(8,128)(2,1)}), bf16[4096,2,1296]{0,2,1:T(8,128)(2,1)}) %all-gather.5.cloned.1.call-update) | async-done | bytes 21233680 | tf_op jit(solution)/shard_map/all_gather | solution.py:43
  572.1 22.7 %fusion.45 = (bf16[768,2,1296]{0,2,1:T(8,128)(2,1)}, f32[768,2,1296]{0,2,1:T(8,128)S(1)}) fusion(bf16[4096,2,1296]{0,2,1:T(8,128)(2,1)} %all-gather.5.cloned.1.call-done, bf16[768,4096]{1,0:T(8,128)(2,1)} %all-gather.3.cloned.1.call-done), kind=kOutput, calls=%fused_computation.110 | convolution fusion | flops 16309444608 | bytes 39469056 | tf_op jit(solution)/shard_map/td,dgc->tgc/dot_general | solution.py:44
  598.3 7.9 collective-permute-start
  608.6 4.3 slice.113
  614.2 14.2 %multiply_convert_fusion.1 = bf16[768,2,1280]{0,2,1:T(8,128)(2,1)} fusion(bf16[768,2,1280]{0,2,1:T(8,128)(2,1)} %slice.113, bf16[3,2,1280]{0,2,1:T(8,128)(2,1)S(1)} %copy.46, f32[2,1280]{1,0:T(2,128)S(1)} %get-tuple-element.31, f32[2,1280]{1,0:T(2,128)S(1)} %get-tuple-element.32, f32[2,1280]{1,0:T(2,128)S(1)} %get-tuple-element.33, ...), kind=kLoop, calls=%fused_computation.3 | loop fusion | flops 51118080 | bytes 7930880 | tf_op jit(solution)/shard_map/convert_element_type | solution.py:52
  628.4 6.3 copy.47
  634.7 3.9 slice.118
  640.5 3.5 copy.48
  651.8 26.3 %collective-permute-done.6 = f32[2,16,64,128]{3,2,1,0:T(8,128)} collective-permute-done((f32[2,16,64,128]{3,2,1,0:T(8,128)S(1)}, f32[2,16,64,128]{3,2,1,0:T(8,128)}, u32[]{:S(2)}, u32[]{:S(2)}) %collective-permute-start.6) | collective-permute-done | bytes 1048608 | tf_op jit(solution)/shard_map/ppermute | solution.py:19
  678.0 3.9 collective-permute-start.7
  682.0 5.4 collective-permute-start.1
  687.4 21.5 %collective-permute-done.1 = f32[2,16]{1,0:T(2,128)S(1)} collective-permute-done((f32[2,16]{1,0:T(2,128)}, f32[2,16]{1,0:T(2,128)S(1)}, u32[]{:S(2)}, u32[]{:S(2)}) %collective-permute-start.1) | collective-permute-done | bytes 160 | tf_op jit(solution)/shard_map/ppermute | solution.py:19
  710.9 3.9 collective-permute-start.8
  718.6 22.0 %collective-permute-done.2 = f32[2,16]{1,0:T(2,128)S(1)} collective-permute-done((f32[2,16]{1,0:T(2,128)}, f32[2,16]{1,0:T(2,128)S(1)}, u32[]{:S(2)}, u32[]{:S(2)}) %collective-permute-start.2) | collective-permute-done | bytes 160 | tf_op jit(solution)/shard_map/ppermute | solution.py:19
  750.1 7.7 collective-permute-done.3
  758.5 3.1 collective-permute-start.4
  763.2 3.2 collective-permute-done.4
  785.7 17.3 %collective-permute-done.10 = f32[2,16,64,128]{3,2,1,0:T(8,128)S(1)} collective-permute-done((f32[2,16,64,128]{3,2,1,0:T(8,128)S(1)}, f32[2,16,64,128]{3,2,1,0:T(8,128)S(1)}, u32[]{:S(2)}, u32[]{:S(2)}) %collective-permute-start.10) | collective-permute-done | bytes 1048608 | tf_op jit(solution)/shard_map/ppermute | solution.py:19
  805.7 8.7 %fusion = f32[6,2,16,64,128]{4,3,2,1,0:T(8,128)} fusion(bf16[6,128,2,16,64]{1,4,3,2,0:T(8,128)(2,1)S(1)} %bitcast.132, f32[6,2,16,128]{3,2,1,0:T(8,128)S(1)} %copy-done.9, f32[6,2,16,128]{3,2,1,0:T(8,128)S(1)} %copy-done.8, f32[6,2,128,128]{3,2,1,0:T(8,128)S(1)} %fusion.32, pred[128,128]{1,0:T(8,128)(4,1)S(1)} %copy-done.10), kind=kOutput, calls=%fused_computation.4 | convolution fusion | flops 421527552 | bytes 10436608 | tf_op jit(solution)/shard_map/qghij,qjghp->qighp/dot_general | solution.py:86
  814.4 7.7 collective-permute-done.11
  822.4 4.4 multiply_reduce_fusion
  826.7 5.6 copy.58
  833.4 2.9 copy.59
  (125 shorter events, 60.6 us)
Async XLA Ops:
  6.5 51.8 %all-gather.3.cloned.1.call-start = ((), (), s32[]{:S(2)}) async-start(), calls=%async_computation | async-start | bytes 7864320 | tf_op jit(solution)/shard_map/all_gather | solution.py:99
  7.3 564.8 %all-gather.5.cloned.1.call-start = ((), (), s32[]{:S(2)}) async-start(), calls=%async_computation.1 | async-start | bytes 21897216 | tf_op jit(solution)/shard_map/all_gather | solution.py:43
  9.7 585.0 %copy-start.22 = (f32[2,16]{1,0:T(2,128)S(1)}, f32[2,16]{1,0:T(2,128)}, u32[]{:S(2)}) copy-start(f32[2,16]{1,0:T(2,128)} %param.12) | copy-start | bytes 388
  598.3 15.5 %collective-permute-start = (bf16[3,2,1280]{2,1,0:T(2,128)(2,1)S(1)}, bf16[3,2,1280]{2,1,0:T(2,128)(2,1)S(1)}, u32[]{:S(2)}, u32[]{:S(2)}) collective-permute-start(bf16[3,2,1280]{2,1,0:T(2,128)(2,1)S(1)} %copy.45), channel_id=1, source_target_pairs={{0,4},{4,8},{8,12},{12,16},{16,20},{20,24},{24,28},{28,32},{32,36}... | collective-permute-start | bytes 46088 | tf_op jit(solution)/shard_map/ppermute | solution.py:19
  608.6 37.5 %copy-start.13 = (f32[2,16]{1,0:T(2,128)}, f32[2,16]{1,0:T(2,128)S(1)}, u32[]{:S(2)}) copy-start(f32[2,16]{1,0:T(2,128)S(1)} %get-tuple-element.21) | copy-start | bytes 388
  608.6 37.5 %copy-start.15 = (f32[2,16]{1,0:T(2,128)}, f32[2,16]{1,0:T(2,128)S(1)}, u32[]{:S(2)}) copy-start(f32[2,16]{1,0:T(2,128)S(1)} %get-tuple-element.22) | copy-start | bytes 388
  649.3 28.8 %collective-permute-start.6 = (f32[2,16,64,128]{3,2,1,0:T(8,128)S(1)}, f32[2,16,64,128]{3,2,1,0:T(8,128)}, u32[]{:S(2)}, u32[]{:S(2)}) collective-permute-start(f32[2,16,64,128]{3,2,1,0:T(8,128)S(1)} %fusion.22), channel_id=1, source_target_pairs={{0,4},{4,8},{8,12},{12,16},{16,20},{20,24},{24,28},{28,32},{32,36}... | collective-permute-start | bytes 3145736 | tf_op jit(solution)/shard_map/ppermute | solution.py:19
  678.0 31.5 %collective-permute-start.7 = (f32[2,16,64,128]{3,2,1,0:T(8,128)}, f32[2,16,64,128]{3,2,1,0:T(8,128)S(1)}, u32[]{:S(2)}, u32[]{:S(2)}) collective-permute-start(f32[2,16,64,128]{3,2,1,0:T(8,128)} %collective-permute-done.6), channel_id=1, source_target_pairs={{0,4},{4,8},{8,12},{12,16},{16,20},{20,24},{24,28},{28,32},{32,36}... | collective-permute-start | bytes 3145736 | tf_op jit(solution)/shard_map/ppermute | solution.py:19
  682.0 26.9 %collective-permute-start.1 = (f32[2,16]{1,0:T(2,128)}, f32[2,16]{1,0:T(2,128)S(1)}, u32[]{:S(2)}, u32[]{:S(2)}) collective-permute-start(f32[2,16]{1,0:T(2,128)} %get-tuple-element.25), channel_id=1, source_target_pairs={{0,4},{4,8},{8,12},{12,16},{16,20},{20,24},{24,28},{28,32},{32,36}... | collective-permute-start | bytes 392 | tf_op jit(solution)/shard_map/ppermute | solution.py:19
  710.9 30.9 %copy-start.4 = (f32[2,16,64,128]{3,2,1,0:T(8,128)}, f32[2,16,64,128]{3,2,1,0:T(8,128)S(1)}, u32[]{:S(2)}) copy-start(f32[2,16,64,128]{3,2,1,0:T(8,128)S(1)} %add_select_fusion.4) | copy-start | bytes 3145732
  710.9 30.9 %collective-permute-start.8 = (f32[2,16,64,128]{3,2,1,0:T(8,128)S(1)}, f32[2,16,64,128]{3,2,1,0:T(8,128)}, u32[]{:S(2)}, u32[]{:S(2)}) collective-permute-start(f32[2,16,64,128]{3,2,1,0:T(8,128)S(1)} %add_select_fusion.4), channel_id=1, source_target_pairs={{0,8},{4,12},{8,16},{12,20},{16,24},{20,28},{24,32},{28,36},{32,40... | collective-permute-start | bytes 3145736 | tf_op jit(solution)/shard_map/ppermute | solution.py:19
  714.8 67.1 %slice-start = ((s8[6291456]{0:T(1024)(128)(4,1)}), s8[2097152]{0:T(1024)(128)(4,1)S(1)}, s32[]{:S(2)}) async-start(s8[6291456]{0:T(1024)(128)(4,1)} %bitcast.128), calls=%async_computation.2 | async-start | bytes 4194304
  715.9 24.6 %collective-permute-start.2 = (f32[2,16]{1,0:T(2,128)}, f32[2,16]{1,0:T(2,128)S(1)}, u32[]{:S(2)}, u32[]{:S(2)}) collective-permute-start(f32[2,16]{1,0:T(2,128)} %broadcast_select_fusion), channel_id=1, source_target_pairs={{0,4},{4,8},{8,12},{12,16},{16,20},{20,24},{24,28},{28,32},{32,36}... | collective-permute-start | bytes 392 | tf_op jit(solution)/shard_map/ppermute | solution.py:19
  743.5 32.3 %collective-permute-start.9 = (f32[2,16,64,128]{3,2,1,0:T(8,128)S(1)}, f32[2,16,64,128]{3,2,1,0:T(8,128)}, u32[]{:S(2)}, u32[]{:S(2)}) collective-permute-start(f32[2,16,64,128]{3,2,1,0:T(8,128)S(1)} %add_select_fusion.3), channel_id=1, source_target_pairs={{0,16},{4,20},{8,24},{12,28},{16,32},{20,36},{24,40},{28,44},{32,4... | collective-permute-start | bytes 3145736 | tf_op jit(solution)/shard_map/ppermute | solution.py:19
  746.1 11.7 %collective-permute-start.3 = (f32[2,16]{1,0:T(2,128)}, f32[2,16]{1,0:T(2,128)}, u32[]{:S(2)}, u32[]{:S(2)}) collective-permute-start(f32[2,16]{1,0:T(2,128)} %multiply_select_fusion.3), channel_id=1, source_target_pairs={{0,8},{4,12},{8,16},{12,20},{16,24},{20,28},{24,32},{28,36},{32,40... | collective-permute-start | bytes 392 | tf_op jit(solution)/shard_map/ppermute | solution.py:19
  758.5 7.9 collective-permute-start.4
  766.9 5.7 collective-permute-start.5
  777.3 25.8 %collective-permute-start.10 = (f32[2,16,64,128]{3,2,1,0:T(8,128)S(1)}, f32[2,16,64,128]{3,2,1,0:T(8,128)S(1)}, u32[]{:S(2)}, u32[]{:S(2)}) collective-permute-start(f32[2,16,64,128]{3,2,1,0:T(8,128)S(1)} %add_select_fusion.2), channel_id=1, source_target_pairs={{0,32},{4,36},{8,40},{12,44},{16,48},{20,52},{24,56},{28,60},{32,6... | collective-permute-start | bytes 3145736 | tf_op jit(solution)/shard_map/ppermute | solution.py:19
  783.1 22.1 %copy-start.5 = (bf16[6,128,2,128]{3,1,0,2:T(8,128)(2,1)S(1)}, bf16[6,128,2,128]{3,1,0,2:T(8,128)(2,1)}, u32[]{:S(2)}) copy-start(bf16[6,128,2,128]{3,1,0,2:T(8,128)(2,1)} %get-tuple-element.11) | copy-start | bytes 1179652
  783.2 22.5 %copy-start.2 = (bf16[6,128,2,1024]{1,3,2,0:T(8,128)(2,1)S(1)}, bf16[6,128,2,1024]{1,3,2,0:T(8,128)(2,1)}, u32[]{:S(2)}) copy-start(bf16[6,128,2,1024]{1,3,2,0:T(8,128)(2,1)} %copy-done.1) | copy-start | bytes 9437188
  783.2 22.5 %copy-start.8 = (f32[6,2,16,128]{3,2,1,0:T(8,128)S(1)}, f32[6,2,16,128]{3,2,1,0:T(8,128)}, u32[]{:S(2)}) copy-start(f32[6,2,16,128]{3,2,1,0:T(8,128)} %copy.52) | copy-start | bytes 294916
  783.2 22.5 %copy-start.9 = (f32[6,2,16,128]{3,2,1,0:T(8,128)S(1)}, f32[6,2,16,128]{3,2,1,0:T(8,128)}, u32[]{:S(2)}) copy-start(f32[6,2,16,128]{3,2,1,0:T(8,128)} %copy.54) | copy-start | bytes 294916
  783.2 22.5 %copy-start.10 = (pred[128,128]{1,0:T(8,128)(4,1)S(1)}, pred[128,128]{1,0:T(8,128)(4,1)}, u32[]{:S(2)}) copy-start(pred[128,128]{1,0:T(8,128)(4,1)} %iota_compare_fusion) | copy-start | bytes 49156
  803.9 18.2 %collective-permute-start.11 = (f32[2,16,64,128]{3,2,1,0:T(8,128)S(1)}, f32[2,16,64,128]{3,2,1,0:T(8,128)S(1)}, u32[]{:S(2)}, u32[]{:S(2)}) collective-permute-start(f32[2,16,64,128]{3,2,1,0:T(8,128)S(1)} %add_select_fusion.1), channel_id=1, source_target_pairs={{0,64},{4,68},{8,72},{12,76},{16,80},{20,84},{24,88},{28,92},{32,9... | collective-permute-start | bytes 3145736 | tf_op jit(solution)/shard_map/ppermute | solution.py:19
  (18 other events, 198.3 us)
Sparse Core Ops, SparseCore 0:
  9.0 49.2 all-gather.2
  59.9 512.1 all-gather.4
where the time goes:
time: 844 us; the launch traced here: 843 us
  waiting for transfers between devices  671 us (80%)
  local copies, waits for them, and re-layouts  43 us (5%)
  other arithmetic  38.9 us (5%)
  matrix products  38.1 us (5%)
  starting transfers between devices  37.9 us (4%)
  between operations  14 us (2%)
    all_gather x1, waiting for transfers between devices, mix_groups(): full_w = lax.all_gather(rows_first, 'seq', axis=0, tiled=True)  514 us
    ppermute x12, waiting for transfers between devices, shifted(): return lax.ppermute(block, axis, route)  108 us
    all_gather x1, waiting for transfers between devices, per_device(): gathered = lax.all_gather(tokens, 'chan', axis=1, tiled=True)  48.6 us
    ppermute x12, starting transfers between devices, shifted(): return lax.ppermute(block, axis, route)  37.8 us
    dot_general x1, matrix products, mix_groups(): jnp.einsum('td,dgc->tgc', gathered, full_w, preferred_element_type=jnp.fl...  22.7 us
  transfers between devices with their start and end apart: 14, of which 10 were waited for; matrix products, arithmetic and copies ran while one was open for 5% of the time, Pallas kernels for 0%

commit v1 on v0

--- a/solution.py
+++ b/solution.py
@@ -96,7 +96,9 @@
 
 
 def per_device(tokens, w_in, conv_w, conv_b, dt_bias, a_log, d_skip, norm_gain):
-    gathered = lax.all_gather(tokens, "chan", axis=1, tiled=True)
+    gathered = jnp.concatenate(
+        lax.all_to_all(jnp.stack([tokens] * lax.axis_size("chan")), "chan", 0, 0), axis=1
+    )
     return mix_groups(gathered, w_in, conv_w, conv_b, dt_bias, a_log, d_skip, norm_gain)
 
 

time: 844 us -> 807 us (0.956)
  waiting for transfers between devices: 671 us -> 609 us
  local copies, waits for them, and re-layouts: 43 us -> 68.4 us
    all_gather x1, waiting for transfers between devices: 514 us -> 295 us  [mix_groups(): full_w = lax.all_gather(rows_first, 'seq', axis=0, tiled=True)]
    all_to_all x0 -> x1, waiting for transfers between devices: none -> 199 us  [per_device(): lax.all_to_all(jnp.stack([tokens] * lax.axis_size('chan')), 'chan', 0, 0)]
    all_gather x1 -> x0, waiting for transfers between devices: 48.6 us -> none  [per_device(): gathered = lax.all_gather(tokens, 'chan', axis=1, tiled=True)]
    reshape x0 -> x2, local copies, waits for them, and re-layouts: none -> 21.4 us  [per_device(): jnp.concatenate(lax.all_to_all(jnp.stack([tokens] * lax.axis_size('chan')...]
  transfers between devices with their start and end apart: 14 -> 14, of which waited for: 10 -> 11; matrix products, arithmetic and copies ran while one was open for 5% -> 8% of each run, Pallas kernels for 0% -> 0%
where the time goes in v1:
time: 807 us; the launch traced here: 804 us
  waiting for transfers between devices  609 us (75%)
  local copies, waits for them, and re-layouts  68.4 us (8%)
  other arithmetic  38.3 us (5%)
  matrix products  38.1 us (5%)
  starting transfers between devices  36.7 us (5%)
  between operations  14 us (2%)
    all_gather x1, waiting for transfers between devices, mix_groups(): full_w = lax.all_gather(rows_first, 'seq', axis=0, tiled=True)  295 us
    all_to_all x1, waiting for transfers between devices, per_device(): lax.all_to_all(jnp.stack([tokens] * lax.axis_size('chan')), 'chan', 0, 0)  199 us
    ppermute x12, waiting for transfers between devices, shifted(): return lax.ppermute(block, axis, route)  114 us
    ppermute x12, starting transfers between devices, shifted(): return lax.ppermute(block, axis, route)  31.3 us
    dot_general x1, matrix products, mix_groups(): jnp.einsum('td,dgc->tgc', gathered, full_w, preferred_element_type=jnp.fl...  22.7 us
    reshape x2, local copies, waits for them, and re-layouts, per_device(): jnp.concatenate(lax.all_to_all(jnp.stack([tokens] * lax.axis_size('chan')...  21.4 us
  transfers between devices with their start and end apart: 14, of which 11 were waited for; matrix products, arithmetic and copies ran while one was open for 8% of the time, Pallas kernels for 0%

profile of v1, /device:TPU:80, one launch (start us, length us, event | category | flops | bytes accessed | tf_op | source)
XLA Modules:
  0.0 804.5 jit_solution(8798290046050220265)
XLA Ops:
  7.3 4.9 stack.6
  12.2 5.4 all-to-all-start
  17.7 199.2 %all-to-all-done = bf16[4,768,1024]{2,1,0:T(8,128)(2,1)} async-done(((bf16[4,768,1024]{2,1,0:T(8,128)(2,1)}), bf16[4,768,1024]{2,1,0:T(8,128)(2,1)}, u32[]{:S(2)}, u32[]{:S(2)}) %all-to-all-start) | async-done | bytes 6291488 | tf_op jit(solution)/shard_map/all_to_all | solution.py:100
  216.9 10.3 %copy.45 = bf16[768,4,1024]{2,1,0:T(4,128)(2,1)} copy(bf16[768,4,1024]{2,0,1:T(8,128)(2,1)} %bitcast) | data formatting | bytes 12582912 | tf_op jit(solution)/shard_map/reshape | solution.py:99
  227.2 11.1 %reshape.86 = bf16[768,4096,1]{1,0,2:T(8,128)(2,1)} reshape(bf16[768,4,1024]{2,1,0:T(4,128)(2,1)} %copy.45) | data formatting | bytes 12582912 | tf_op jit(solution)/shard_map/reshape | solution.py:99
  238.3 294.7 %all-gather.2.cloned.1.call-done = bf16[4096,2,1296]{0,2,1:T(8,128)(2,1)} async-done(((bf16[128,2,1296]{0,2,1:T(8,128)(2,1)}), bf16[4096,2,1296]{0,2,1:T(8,128)(2,1)}) %all-gather.2.cloned.1.call-update) | async-done | bytes 21233680 | tf_op jit(solution)/shard_map/all_gather | solution.py:43
  533.0 22.7 %fusion.43 = (bf16[768,2,1296]{0,2,1:T(8,128)(2,1)}, f32[768,2,1296]{0,2,1:T(8,128)S(1)}) fusion(bf16[768,4096,1]{1,0,2:T(8,128)(2,1)} %reshape.86, bf16[4096,2,1296]{0,2,1:T(8,128)(2,1)} %all-gather.2.cloned.1.call-done), kind=kOutput, calls=%fused_computation.108 | convolution fusion | flops 16309444608 | bytes 39469056 | tf_op jit(solution)/shard_map/td,dgc->tgc/dot_general | solution.py:44
  564.5 4.3 slice.113
  570.1 14.3 %multiply_convert_fusion.1 = bf16[768,2,1280]{0,2,1:T(8,128)(2,1)} fusion(bf16[768,2,1280]{0,2,1:T(8,128)(2,1)} %slice.113, bf16[3,2,1280]{0,2,1:T(8,128)(2,1)S(1)} %copy.47, f32[2,1280]{1,0:T(2,128)S(1)} %get-tuple-element.31, f32[2,1280]{1,0:T(2,128)S(1)} %get-tuple-element.32, f32[2,1280]{1,0:T(2,128)S(1)} %get-tuple-element.33, ...), kind=kLoop, calls=%fused_computation.3 | loop fusion | flops 51118080 | bytes 7930880 | tf_op jit(solution)/shard_map/convert_element_type | solution.py:52
  584.4 6.4 copy.48
  590.8 3.9 slice.118
  596.6 3.5 copy.49
  607.2 28.3 %collective-permute-done.6 = f32[2,16,64,128]{3,2,1,0:T(8,128)} collective-permute-done((f32[2,16,64,128]{3,2,1,0:T(8,128)S(1)}, f32[2,16,64,128]{3,2,1,0:T(8,128)}, u32[]{:S(2)}, u32[]{:S(2)}) %collective-permute-start.6) | collective-permute-done | bytes 1048608 | tf_op jit(solution)/shard_map/ppermute | solution.py:19
  639.4 25.5 %collective-permute-done.1 = f32[2,16]{1,0:T(2,128)S(1)} collective-permute-done((f32[2,16]{1,0:T(2,128)}, f32[2,16]{1,0:T(2,128)S(1)}, u32[]{:S(2)}, u32[]{:S(2)}) %collective-permute-start.1) | collective-permute-done | bytes 160 | tf_op jit(solution)/shard_map/ppermute | solution.py:19
  672.6 18.6 %collective-permute-done.2 = f32[2,16]{1,0:T(2,128)S(1)} collective-permute-done((f32[2,16]{1,0:T(2,128)}, f32[2,16]{1,0:T(2,128)S(1)}, u32[]{:S(2)}, u32[]{:S(2)}) %collective-permute-start.2) | collective-permute-done | bytes 160 | tf_op jit(solution)/shard_map/ppermute | solution.py:19
  702.7 15.3 %collective-permute-done.3 = f32[2,16]{1,0:T(2,128)} collective-permute-done((f32[2,16]{1,0:T(2,128)}, f32[2,16]{1,0:T(2,128)}, u32[]{:S(2)}, u32[]{:S(2)}) %collective-permute-start.3) | collective-permute-done | bytes 160 | tf_op jit(solution)/shard_map/ppermute | solution.py:19
  718.7 6.1 collective-permute-start.4
  727.1 3.5 collective-permute-start.5
  737.4 3.5 collective-permute-start.10
  747.3 12.3 %collective-permute-done.10 = f32[2,16,64,128]{3,2,1,0:T(8,128)S(1)} collective-permute-done((f32[2,16,64,128]{3,2,1,0:T(8,128)S(1)}, f32[2,16,64,128]{3,2,1,0:T(8,128)S(1)}, u32[]{:S(2)}, u32[]{:S(2)}) %collective-permute-start.10) | collective-permute-done | bytes 1048608 | tf_op jit(solution)/shard_map/ppermute | solution.py:19
  762.6 8.7 %fusion = f32[6,2,16,64,128]{4,3,2,1,0:T(8,128)} fusion(bf16[6,128,2,16,64]{1,4,3,2,0:T(8,128)(2,1)S(1)} %bitcast.129, f32[6,2,16,128]{3,2,1,0:T(8,128)S(1)} %copy-done.9, f32[6,2,16,128]{3,2,1,0:T(8,128)S(1)} %copy-done.8, f32[6,2,128,128]{3,2,1,0:T(8,128)S(1)} %fusion.30, pred[128,128]{1,0:T(8,128)(4,1)S(1)} %copy-done.11), kind=kOutput, calls=%fused_computation.4 | convolution fusion | flops 421527552 | bytes 10436608 | tf_op jit(solution)/shard_map/qghij,qjghp->qighp/dot_general | solution.py:86
  771.3 12.2 %collective-permute-done.11 = f32[2,16,64,128]{3,2,1,0:T(8,128)S(1)} collective-permute-done((f32[2,16,64,128]{3,2,1,0:T(8,128)S(1)}, f32[2,16,64,128]{3,2,1,0:T(8,128)S(1)}, u32[]{:S(2)}, u32[]{:S(2)}) %collective-permute-start.11) | collective-permute-done | bytes 1048608 | tf_op jit(solution)/shard_map/ppermute | solution.py:19
  783.7 4.4 multiply_reduce_fusion
  788.0 5.6 copy.59
  (131 shorter events, 66.1 us)
Async XLA Ops:
  6.5 526.5 %all-gather.2.cloned.1.call-start = ((), (), s32[]{:S(2)}) async-start(), calls=%async_computation.1 | async-start | bytes 21897216 | tf_op jit(solution)/shard_map/all_gather | solution.py:43
  12.2 204.7 %all-to-all-start = ((bf16[4,768,1024]{2,1,0:T(8,128)(2,1)}), bf16[4,768,1024]{2,1,0:T(8,128)(2,1)}, u32[]{:S(2)}, u32[]{:S(2)}) async-start(bf16[4,768,1024]{2,1,0:T(8,128)(2,1)} %stack.6), calls=%async_computation | async-start | bytes 12582912 | tf_op jit(solution)/shard_map/all_to_all | solution.py:100
  238.3 317.3 %copy-start.23 = (f32[2,16]{1,0:T(2,128)S(1)}, f32[2,16]{1,0:T(2,128)}, u32[]{:S(2)}) copy-start(f32[2,16]{1,0:T(2,128)} %param.12) | copy-start | bytes 388
  559.2 10.5 %collective-permute-start = (bf16[3,2,1280]{2,1,0:T(2,128)(2,1)S(1)}, bf16[3,2,1280]{2,1,0:T(2,128)(2,1)S(1)}, u32[]{:S(2)}, u32[]{:S(2)}) collective-permute-start(bf16[3,2,1280]{2,1,0:T(2,128)(2,1)S(1)} %copy.46), channel_id=1, source_target_pairs={{0,4},{4,8},{8,12},{12,16},{16,20},{20,24},{24,28},{28,32},{32,36}... | collective-permute-start | bytes 46088 | tf_op jit(solution)/shard_map/ppermute | solution.py:19
  564.5 37.6 %copy-start.14 = (f32[2,16]{1,0:T(2,128)}, f32[2,16]{1,0:T(2,128)S(1)}, u32[]{:S(2)}) copy-start(f32[2,16]{1,0:T(2,128)S(1)} %get-tuple-element.21) | copy-start | bytes 388
  564.5 37.7 %copy-start.16 = (f32[2,16]{1,0:T(2,128)}, f32[2,16]{1,0:T(2,128)S(1)}, u32[]{:S(2)}) copy-start(f32[2,16]{1,0:T(2,128)S(1)} %get-tuple-element.22) | copy-start | bytes 388
  605.3 30.2 %collective-permute-start.6 = (f32[2,16,64,128]{3,2,1,0:T(8,128)S(1)}, f32[2,16,64,128]{3,2,1,0:T(8,128)}, u32[]{:S(2)}, u32[]{:S(2)}) collective-permute-start(f32[2,16,64,128]{3,2,1,0:T(8,128)S(1)} %fusion.20), channel_id=1, source_target_pairs={{0,4},{4,8},{8,12},{12,16},{16,20},{20,24},{24,28},{28,32},{32,36}... | collective-permute-start | bytes 3145736 | tf_op jit(solution)/shard_map/ppermute | solution.py:19
  635.5 29.9 %collective-permute-start.7 = (f32[2,16,64,128]{3,2,1,0:T(8,128)}, f32[2,16,64,128]{3,2,1,0:T(8,128)S(1)}, u32[]{:S(2)}, u32[]{:S(2)}) collective-permute-start(f32[2,16,64,128]{3,2,1,0:T(8,128)} %collective-permute-done.6), channel_id=1, source_target_pairs={{0,4},{4,8},{8,12},{12,16},{16,20},{20,24},{24,28},{28,32},{32,36}... | collective-permute-start | bytes 3145736 | tf_op jit(solution)/shard_map/ppermute | solution.py:19
  637.5 27.4 %collective-permute-start.1 = (f32[2,16]{1,0:T(2,128)}, f32[2,16]{1,0:T(2,128)S(1)}, u32[]{:S(2)}, u32[]{:S(2)}) collective-permute-start(f32[2,16]{1,0:T(2,128)} %get-tuple-element.25), channel_id=1, source_target_pairs={{0,4},{4,8},{8,12},{12,16},{16,20},{20,24},{24,28},{28,32},{32,36}... | collective-permute-start | bytes 392 | tf_op jit(solution)/shard_map/ppermute | solution.py:19
  666.9 25.5 %copy-start.4 = (f32[2,16,64,128]{3,2,1,0:T(8,128)}, f32[2,16,64,128]{3,2,1,0:T(8,128)S(1)}, u32[]{:S(2)}) copy-start(f32[2,16,64,128]{3,2,1,0:T(8,128)S(1)} %add_select_fusion.4) | copy-start | bytes 3145732
  666.9 27.3 %collective-permute-start.8 = (f32[2,16,64,128]{3,2,1,0:T(8,128)S(1)}, f32[2,16,64,128]{3,2,1,0:T(8,128)}, u32[]{:S(2)}, u32[]{:S(2)}) collective-permute-start(f32[2,16,64,128]{3,2,1,0:T(8,128)S(1)} %add_select_fusion.4), channel_id=1, source_target_pairs={{0,8},{4,12},{8,16},{12,20},{16,24},{20,28},{24,32},{28,36},{32,40... | collective-permute-start | bytes 3145736 | tf_op jit(solution)/shard_map/ppermute | solution.py:19
  668.8 74.8 %slice-start = ((s8[6291456]{0:T(1024)(128)(4,1)}), s8[2097152]{0:T(1024)(128)(4,1)S(1)}, s32[]{:S(2)}) async-start(s8[6291456]{0:T(1024)(128)(4,1)} %bitcast.125), calls=%async_computation.2 | async-start | bytes 4194304
  669.9 21.2 %collective-permute-start.2 = (f32[2,16]{1,0:T(2,128)}, f32[2,16]{1,0:T(2,128)S(1)}, u32[]{:S(2)}, u32[]{:S(2)}) collective-permute-start(f32[2,16]{1,0:T(2,128)} %broadcast_select_fusion), channel_id=1, source_target_pairs={{0,4},{4,8},{8,12},{12,16},{16,20},{20,24},{24,28},{28,32},{32,36}... | collective-permute-start | bytes 392 | tf_op jit(solution)/shard_map/ppermute | solution.py:19
  695.9 40.0 %collective-permute-start.9 = (f32[2,16,64,128]{3,2,1,0:T(8,128)S(1)}, f32[2,16,64,128]{3,2,1,0:T(8,128)}, u32[]{:S(2)}, u32[]{:S(2)}) collective-permute-start(f32[2,16,64,128]{3,2,1,0:T(8,128)S(1)} %add_select_fusion.3), channel_id=1, source_target_pairs={{0,16},{4,20},{8,24},{12,28},{16,32},{20,36},{24,40},{28,44},{32,4... | collective-permute-start | bytes 3145736 | tf_op jit(solution)/shard_map/ppermute | solution.py:19
  698.5 19.5 %collective-permute-start.3 = (f32[2,16]{1,0:T(2,128)}, f32[2,16]{1,0:T(2,128)}, u32[]{:S(2)}, u32[]{:S(2)}) collective-permute-start(f32[2,16]{1,0:T(2,128)} %multiply_select_fusion.3), channel_id=1, source_target_pairs={{0,8},{4,12},{8,16},{12,20},{16,24},{20,28},{24,32},{28,36},{32,40... | collective-permute-start | bytes 392 | tf_op jit(solution)/shard_map/ppermute | solution.py:19
  718.7 7.9 collective-permute-start.4
  727.1 5.6 collective-permute-start.5
  737.4 22.3 %collective-permute-start.10 = (f32[2,16,64,128]{3,2,1,0:T(8,128)S(1)}, f32[2,16,64,128]{3,2,1,0:T(8,128)S(1)}, u32[]{:S(2)}, u32[]{:S(2)}) collective-permute-start(f32[2,16,64,128]{3,2,1,0:T(8,128)S(1)} %add_select_fusion.2), channel_id=1, source_target_pairs={{0,32},{4,36},{8,40},{12,44},{16,48},{20,52},{24,56},{28,60},{32,6... | collective-permute-start | bytes 3145736 | tf_op jit(solution)/shard_map/ppermute | solution.py:19
  760.5 22.9 %collective-permute-start.11 = (f32[2,16,64,128]{3,2,1,0:T(8,128)S(1)}, f32[2,16,64,128]{3,2,1,0:T(8,128)S(1)}, u32[]{:S(2)}, u32[]{:S(2)}) collective-permute-start(f32[2,16,64,128]{3,2,1,0:T(8,128)S(1)} %add_select_fusion.1), channel_id=1, source_target_pairs={{0,64},{4,68},{8,72},{12,76},{16,80},{20,84},{24,88},{28,92},{32,9... | collective-permute-start | bytes 3145736 | tf_op jit(solution)/shard_map/ppermute | solution.py:19
  762.1 21.5 %slice-start.2 = ((s8[6291456]{0:T(1024)(128)(4,1)}), s8[4194304]{0:T(1024)(128)(4,1)S(1)}, s32[]{:S(2)}) async-start(s8[6291456]{0:T(1024)(128)(4,1)} %bitcast.133), calls=%async_computation.4 | async-start | bytes 8388608
  762.5 21.1 %slice-start.3 = ((s8[6291456]{0:T(1024)(128)(4,1)}), s8[2097152]{0:T(1024)(128)(4,1)S(1)}, s32[]{:S(2)}) async-start(s8[6291456]{0:T(1024)(128)(4,1)} %bitcast.133), calls=%async_computation.5 | async-start | bytes 4194304
  762.5 21.1 %copy-start.7 = (f32[6,128,2,16]{1,3,2,0:T(8,128)S(1)}, f32[6,128,2,16]{1,3,2,0:T(8,128)}, u32[]{:S(2)}) copy-start(f32[6,128,2,16]{1,3,2,0:T(8,128)} %copy.56) | copy-start | bytes 294916
  762.5 21.1 %copy-start.20 = (f32[6,2,16]{2,1,0:T(2,128)S(1)}, f32[6,2,16]{2,1,0:T(2,128)}, u32[]{:S(2)}) copy-start(f32[6,2,16]{2,1,0:T(2,128)} %copy-done.19) | copy-start | bytes 2308
  762.5 21.1 %copy-start.24 = (f32[2,16]{1,0:T(2,128)S(1)}, f32[2,16]{1,0:T(2,128)}, u32[]{:S(2)}) copy-start(f32[2,16]{1,0:T(2,128)} %param.14) | copy-start | bytes 388
  (20 other events, 206.2 us)
Sparse Core Ops, SparseCore 0:
  8.9 524.0 all-gather.1
